TPU v7x, 32 devices: a whole 2x2x4 slice. The times are simulated.
32 devices in a mesh: strip: 8 (over z, x), chan: 4 (over y, core).
Axes of the slice: x: 2, y: 2, z: 4, core: 2. Of those that a mesh axis runs over, the one named last changes fastest.
Arguments:
- features: bfloat16 [512, 32, 128], P('chan', 'strip'), may hold values from -6 to 6
- first_filters: bfloat16 [512, 3, 3, 512], P('chan'), may hold values from -0.09375 to 0.09375
- second_filters: bfloat16 [512, 3, 3, 512], P('chan'), may hold values from -0.09375 to 0.09375
- out_grad: bfloat16 [512, 32, 128], P('chan', 'strip'), may hold values from -6 to 6
Outputs:
- output: bfloat16 [512, 32, 128], P('chan', 'strip')
- input_grad: bfloat16 [512, 32, 128], P('chan', 'strip')
- first_grad: float32 [512, 3, 3, 512], P('chan')
- second_grad: float32 [512, 3, 3, 512], P('chan')
All inputs are finite; a program needn't handle non-finite values.
Results may differ from a plain program's by a relative error of at most 0.005.
Values may be sent and summed in bfloat16 or wider, within the bound.
No kernel may reach another device: no remote copies, remote signals or barrier semaphores. Data moves between devices by JAX's collectives and lax.ppermute only.
A program may use at most 128 MiB of HBM per device.

v0:
```python
import jax
import jax.numpy as jnp
from jax import lax
from jax.sharding import PartitionSpec as P


def extended(cells, sides, width):
    for axis, dim in sides:
        count = lax.axis_size(axis)
        ends = count - 1
        head = lax.slice_in_dim(cells, 0, width, axis=dim)
        tail = lax.slice_in_dim(cells, cells.shape[dim] - width, cells.shape[dim], axis=dim)
        cells = jnp.concatenate(
            [
                lax.ppermute(tail, axis, [(i, (i + 1) % count) for i in range(ends)]),
                cells,
                lax.ppermute(head, axis, [((i + 1) % count, i) for i in range(ends)]),
            ],
            axis=dim,
        )
    return cells


def take_cols(field, shift):
    if shift == 0:
        return field
    edge = jnp.zeros(field.shape[:-1] + (1,), field.dtype)
    if shift > 0:
        return jnp.concatenate([field[..., 1:], edge], axis=-1)
    return jnp.concatenate([edge, field[..., :-1]], axis=-1)


def conv_fwd(padded, weight):
    chans, rows_pad, cols = padded.shape
    rows = rows_pad - 2
    outs = weight.shape[0]
    flat_w = weight.reshape(outs * 9, chans)
    taps = jnp.dot(
        flat_w, padded.reshape(chans, rows_pad * cols), preferred_element_type=jnp.float32
    )
    taps = taps.reshape(outs, 3, 3, rows_pad, cols)
    total = jnp.zeros((outs, rows, cols), jnp.float32)
    for kh in range(3):
        for kw in range(3):
            total = total + take_cols(taps[:, kh, kw, kh : kh + rows, :], kw - 1)
    return total


def back_stack(padded):
    outs, rows_pad, cols = padded.shape
    rows = rows_pad - 2
    pieces = []
    for kh in range(3):
        for kw in range(3):
            pieces.append(take_cols(padded[:, 2 - kh : 2 - kh + rows, :], 1 - kw))
    return jnp.stack(pieces, axis=1).reshape(outs * 9, rows * cols)


def conv_back_stacked(stacked, weight, rows, cols):
    outs = weight.shape[0]
    inner = weight.shape[3]
    flat_w = weight.reshape(outs * 9, inner)
    result = lax.dot_general(
        flat_w, stacked, (((0,), (0,)), ((), ())), preferred_element_type=jnp.float32
    )
    return result.reshape(inner, rows, cols)


def filter_grad(grad_out, padded):
    outs, rows, cols = grad_out.shape
    chans, rows_pad, _ = padded.shape
    pieces = []
    for kh in range(3):
        for kw in range(3):
            moved = take_cols(grad_out, 1 - kw)
            pieces.append(jnp.pad(moved, ((0, 0), (kh, 2 - kh), (0, 0))))
    stacked = jnp.stack(pieces, axis=1).reshape(outs * 9, rows_pad * cols)
    result = lax.dot_general(
        stacked,
        padded.reshape(chans, rows_pad * cols),
        (((1,), (1,)), ((), ())),
        preferred_element_type=jnp.float32,
    )
    return result.reshape(outs, 3, 3, chans)


def chan_sum_scatter(part, axis):
    count = lax.axis_size(axis)
    me = lax.axis_index(axis)
    blocks = part.reshape((count, part.shape[0] // count) + part.shape[1:])
    bit = 1
    while bit < count:
        pairs = blocks.reshape((blocks.shape[0] // 2, 2) + blocks.shape[1:])
        side = me // bit % 2
        keep = lax.dynamic_index_in_dim(pairs, side, axis=1, keepdims=False)
        send = lax.dynamic_index_in_dim(pairs, 1 - side, axis=1, keepdims=False)
        blocks = keep + lax.ppermute(send, axis, [(i, i ^ bit) for i in range(count)])
        bit *= 2
    return blocks.reshape(blocks.shape[1:])


def body(features, first_filters, second_filters, out_grad):
    blocks, rows, cols = features.shape
    dy_pad = extended(out_grad, (("strip", 1),), 1)
    dy_stack = back_stack(dy_pad)
    hidden_grad = chan_sum_scatter(conv_back_stacked(dy_stack, second_filters, rows, cols), "chan")
    x_pad = extended(features, (("strip", 1),), 1)
    x_all = lax.all_gather(x_pad, "chan", axis=0, tiled=True)
    pre_full = conv_fwd(x_all, first_filters)
    pre = pre_full.astype(jnp.bfloat16)
    hidden = jax.nn.silu(pre_full).astype(jnp.bfloat16)
    h_pad = extended(hidden, (("strip", 1),), 1)
    h_all = lax.all_gather(h_pad, "chan", axis=0, tiled=True)
    second_grad = lax.psum(filter_grad(out_grad, h_all), "strip")
    output = (features.astype(jnp.float32) + conv_fwd(h_all, second_filters)).astype(jnp.bfloat16)
    pre_val = pre.astype(jnp.float32)
    sig = jax.nn.sigmoid(pre_val)
    pre_grad = (hidden_grad * sig * (1.0 + pre_val * (1.0 - sig))).astype(jnp.bfloat16)
    da_pad = extended(pre_grad, (("strip", 1),), 1)
    second_grad, late_grad = lax.optimization_barrier((second_grad, pre_grad))
    first_grad = lax.psum(filter_grad(late_grad, x_all), "strip")
    da_stack = back_stack(da_pad)
    input_term = chan_sum_scatter(conv_back_stacked(da_stack, first_filters, rows, cols), "chan")
    input_grad = (out_grad.astype(jnp.float32) + input_term).astype(jnp.bfloat16)
    return (output, input_grad, first_grad, second_grad)


def solution(mesh):
    in_specs = (
        P("chan", "strip", None),
        P("chan", None, None, None),
        P("chan", None, None, None),
        P("chan", "strip", None),
    )
    out_specs = (
        P("chan", "strip", None),
        P("chan", "strip", None),
        P("chan", None, None, None),
        P("chan", None, None, None),
    )
    return jax.shard_map(body, mesh=mesh, in_specs=in_specs, out_specs=out_specs, check_vma=False)
```

profile of v0, /device:TPU:0, one launch (start us, length us, event | category | flops | bytes accessed | tf_op | source)
XLA Modules:
  0.0 348.0 jit_solution(8642496405318678284)
XLA Ops:
  8.3 4.8 %collective-permute-start.5 = (bf16[128,1,128]{0,2,1:T(8,128)(2,1)S(1)}, bf16[128,1,128]{0,2,1:T(8,128)(2,1)S(1)}, u32[]{:S(2)}, u32[]{:S(2)}) collective-permute-start(bf16[128,1,128]{0,2,1:T(8,128)(2,1)S(1)} %get-tuple-element.42), channel_id=1, source_target_pairs={{0,4},{4,8},{8,12},{12,16},{16,20},{20,24},{24,28},{1,5},{5,9},{9,... | collective-permute-start | bytes 98312 | tf_op jit(solution)/shard_map/ppermute | solution.py:15
  17.4 5.2 %collective-permute-start = (bf16[128,1,128]{0,2,1:T(8,128)(2,1)}, bf16[128,1,128]{0,2,1:T(8,128)(2,1)S(1)}, u32[]{:S(2)}, u32[]{:S(2)}) collective-permute-start(bf16[128,1,128]{0,2,1:T(8,128)(2,1)} %get-tuple-element.36), channel_id=1, source_target_pairs={{0,4},{4,8},{8,12},{12,16},{16,20},{20,24},{24,28},{1,5},{5,9},{9,... | collective-permute-start | bytes 98312 | tf_op jit(solution)/shard_map/ppermute | solution.py:15
  22.6 2.3 copy.93
  26.0 2.7 copy.80
  33.3 3.1 convolution_bitcast_fusion.3
  40.7 8.9 %all_gather.6 = bf16[512,6,128]{0,2,1:T(8,128)(2,1)S(1)} all-gather(bf16[128,6,128]{0,2,1:T(8,128)(2,1)S(1)} %pad_maximum_fusion.1), channel_id=1, replica_groups=mesh['strip'=8,'chan'=4] {'chan'}, dimensions={0}, use_global_device_ids=true | all-gather | bytes 983040 | tf_op jit(solution)/shard_map/all_gather | solution.py:108
  51.0 3.1 convolution_bitcast_fusion.1
  55.5 5.2 %copy.81 = f32[1152,768]{1,0:T(8,128)} copy(f32[1152,768]{0,1:T(8,128)} %convolution_bitcast_fusion.1) | data formatting | bytes 7077888 | tf_op jit(solution)/shard_map/dot_general | solution.py:38
  60.7 4.8 %reshape.62 = f32[128,3,3,6,128]{4,3,2,1,0:T(8,128)} reshape(f32[1152,768]{1,0:T(8,128)} %copy.81) | data formatting | bytes 7077888 | tf_op jit(solution)/shard_map/reshape | solution.py:41
  74.7 4.3 %collective-permute-done.7 = f32[1,128,4,128]{3,2,1,0:T(4,128)S(1)} collective-permute-done((f32[1,128,4,128]{3,2,1,0:T(4,128)S(1)}, f32[1,128,4,128]{3,2,1,0:T(4,128)S(1)}, u32[]{:S(2)}, u32[]{:S(2)}) %collective-permute-start.7) | collective-permute-done | bytes 262176 | tf_op jit(solution)/shard_map/ppermute | solution.py:97
  82.6 5.5 %collective-permute-start.2 = (bf16[128,1,128]{2,1,0:T(2,128)(2,1)S(1)}, bf16[128,1,128]{2,1,0:T(2,128)(2,1)S(1)}, u32[]{:S(2)}, u32[]{:S(2)}) collective-permute-start(bf16[128,1,128]{2,1,0:T(2,128)(2,1)S(1)} %get-tuple-element.34), channel_id=1, source_target_pairs={{0,4},{4,8},{8,12},{12,16},{16,20},{20,24},{24,28},{1,5},{5,9},{9,... | collective-permute-start | bytes 98312 | tf_op jit(solution)/shard_map/ppermute | solution.py:15
  90.2 8.8 %all_gather.7 = bf16[512,6,128]{2,0,1:T(8,128)(2,1)S(1)} all-gather(bf16[128,6,128]{2,0,1:T(8,128)(2,1)S(1)} %copy.91), channel_id=1, replica_groups=mesh['strip'=8,'chan'=4] {'chan'}, dimensions={0}, use_global_device_ids=true | all-gather | bytes 983040 | tf_op jit(solution)/shard_map/all_gather | solution.py:113
  99.3 4.3 %fusion.72 = f32[128,3,3,512]{3,0,2,1:T(8,128)} fusion(bf16[128,3,3,768]{0,3,2,1:T(8,128)(2,1)} %bitcast.57, bf16[512,768,1,1]{0,1,3,2:T(8,128)(2,1)S(1)} %bitcast.264), kind=kOutput, calls=%fused_computation.154 | convolution fusion | flops 905969664 | bytes 4915200 | tf_op jit(solution)/shard_map/dot_general | solution.py:78
  103.8 4.8 %collective-permute-start.9 = (bf16[128,1,128]{2,1,0:T(2,128)(2,1)S(1)}, bf16[128,1,128]{2,1,0:T(2,128)(2,1)S(1)}, u32[]{:S(2)}, u32[]{:S(2)}) collective-permute-start(bf16[128,1,128]{2,1,0:T(2,128)(2,1)S(1)} %get-tuple-element.32), channel_id=1, source_target_pairs={{0,4},{4,8},{8,12},{12,16},{16,20},{20,24},{24,28},{1,5},{5,9},{9,... | collective-permute-start | bytes 98312 | tf_op jit(solution)/shard_map/ppermute | solution.py:15
  110.5 7.2 %collective-permute-done.8 = bf16[128,1,128]{2,1,0:T(2,128)(2,1)S(1)} collective-permute-done((bf16[128,1,128]{2,1,0:T(2,128)(2,1)S(1)}, bf16[128,1,128]{2,1,0:T(2,128)(2,1)S(1)}, u32[]{:S(2)}, u32[]{:S(2)}) %collective-permute-start.8) | collective-permute-done | bytes 32800 | tf_op jit(solution)/shard_map/ppermute | solution.py:17
  119.2 96.3 %all-reduce.47.cloned.1.call-done = f32[128,3,3,512]{3,0,2,1:T(8,128)} async-done(((f32[128,3,3,512]{3,0,2,1:T(8,128)}), f32[128,3,3,512]{3,0,2,1:T(8,128)}) %all-reduce.47.cloned.1.call-update) | async-done | bytes 2359312 | tf_op jit(solution)/shard_map/psum | solution.py:114
  222.9 3.1 copy.121
  226.0 2.5 fusion.73
  235.8 2.7 convolution_bitcast_fusion
  238.6 3.0 copy.94
  241.6 4.9 %reshape.65 = f32[128,3,3,6,128]{4,3,2,1,0:T(8,128)} reshape(f32[1152,768]{1,0:T(8,128)} %copy.94) | data formatting | bytes 7077888 | tf_op jit(solution)/shard_map/reshape | solution.py:41
  253.1 2.6 fusion.21
  258.0 78.5 %all-reduce.49.cloned.1.call-done = f32[128,3,3,512]{3,0,2,1:T(8,128)} async-done(((f32[128,3,3,512]{3,0,2,1:T(8,128)}), f32[128,3,3,512]{3,0,2,1:T(8,128)}) %all-reduce.49.cloned.1.call-update) | async-done | bytes 2359312 | tf_op jit(solution)/shard_map/psum | solution.py:121
  336.5 3.3 copy.190
  (124 shorter events, 61.6 us)
Async XLA Ops:
  7.2 208.3 %all-reduce.47.cloned.1.call-start = ((), (), s32[]{:S(2)}) async-start(), calls=%async_computation | async-start | bytes 4718592 | tf_op jit(solution)/shard_map/psum | solution.py:114
  8.3 22.6 %collective-permute-start.5 = (bf16[128,1,128]{0,2,1:T(8,128)(2,1)S(1)}, bf16[128,1,128]{0,2,1:T(8,128)(2,1)S(1)}, u32[]{:S(2)}, u32[]{:S(2)}) collective-permute-start(bf16[128,1,128]{0,2,1:T(8,128)(2,1)S(1)} %get-tuple-element.42), channel_id=1, source_target_pairs={{0,4},{4,8},{8,12},{12,16},{16,20},{20,24},{24,28},{1,5},{5,9},{9,... | collective-permute-start | bytes 98312 | tf_op jit(solution)/shard_map/ppermute | solution.py:15
  13.1 17.8 %collective-permute-start.4 = (bf16[128,1,128]{0,2,1:T(8,128)(2,1)S(1)}, bf16[128,1,128]{0,2,1:T(8,128)(2,1)S(1)}, u32[]{:S(2)}, u32[]{:S(2)}) collective-permute-start(bf16[128,1,128]{0,2,1:T(8,128)(2,1)S(1)} %get-tuple-element.43), channel_id=1, source_target_pairs={{4,0},{8,4},{12,8},{16,12},{20,16},{24,20},{28,24},{5,1},{9,5},{13... | collective-permute-start | bytes 98312 | tf_op jit(solution)/shard_map/ppermute | solution.py:17
  16.1 24.6 %collective-permute-start.1 = (bf16[128,1,128]{0,2,1:T(8,128)(2,1)}, bf16[128,1,128]{0,2,1:T(8,128)(2,1)S(1)}, u32[]{:S(2)}, u32[]{:S(2)}) collective-permute-start(bf16[128,1,128]{0,2,1:T(8,128)(2,1)} %get-tuple-element.37), channel_id=1, source_target_pairs={{4,0},{8,4},{12,8},{16,12},{20,16},{24,20},{28,24},{5,1},{9,5},{13... | collective-permute-start | bytes 98312 | tf_op jit(solution)/shard_map/ppermute | solution.py:17
  17.4 23.3 %collective-permute-start = (bf16[128,1,128]{0,2,1:T(8,128)(2,1)}, bf16[128,1,128]{0,2,1:T(8,128)(2,1)S(1)}, u32[]{:S(2)}, u32[]{:S(2)}) collective-permute-start(bf16[128,1,128]{0,2,1:T(8,128)(2,1)} %get-tuple-element.36), channel_id=1, source_target_pairs={{0,4},{4,8},{8,12},{12,16},{16,20},{20,24},{24,28},{1,5},{5,9},{9,... | collective-permute-start | bytes 98312 | tf_op jit(solution)/shard_map/ppermute | solution.py:15
  25.9 7.3 %copy-start.1 = (bf16[1152,512]{1,0:T(8,128)(2,1)}, bf16[1152,512]{1,0:T(8,128)(2,1)S(1)}, u32[]{:S(2)}) copy-start(bf16[1152,512]{1,0:T(8,128)(2,1)S(1)} %reshape.64) | copy-start | bytes 3538948
  39.3 11.7 %copy-start.2 = (bf16[1152,512]{1,0:T(8,128)(2,1)S(1)}, bf16[1152,512]{1,0:T(8,128)(2,1)}, u32[]{:S(2)}) copy-start(bf16[1152,512]{1,0:T(8,128)(2,1)} %reshape.61) | copy-start | bytes 3538948
  40.7 28.5 %collective-permute-start.6 = (f32[2,128,4,128]{3,2,1,0:T(4,128)}, f32[2,128,4,128]{3,2,1,0:T(4,128)}, u32[]{:S(2)}, u32[]{:S(2)}) collective-permute-start(f32[2,128,4,128]{3,2,1,0:T(4,128)} %bitcast.33), channel_id=1, source_target_pairs={{0,1},{1,0},{2,3},{3,2},{4,5},{5,4},{6,7},{7,6},{8,9},{9,8},{10,11... | collective-permute-start | bytes 1572872 | tf_op jit(solution)/shard_map/ppermute | solution.py:97
  70.4 8.6 %collective-permute-start.7 = (f32[1,128,4,128]{3,2,1,0:T(4,128)S(1)}, f32[1,128,4,128]{3,2,1,0:T(4,128)S(1)}, u32[]{:S(2)}, u32[]{:S(2)}) collective-permute-start(f32[1,128,4,128]{3,2,1,0:T(4,128)S(1)} %constant_dynamic-slice_fusion.3), channel_id=1, source_target_pairs={{0,2},{1,3},{2,0},{3,1},{4,6},{5,7},{6,4},{7,5},{8,10},{9,11},{10,... | collective-permute-start | bytes 786440 | tf_op jit(solution)/shard_map/ppermute | solution.py:97
  81.3 7.5 %collective-permute-start.3 = (bf16[128,1,128]{2,1,0:T(2,128)(2,1)S(1)}, bf16[128,1,128]{2,1,0:T(2,128)(2,1)S(1)}, u32[]{:S(2)}, u32[]{:S(2)}) collective-permute-start(bf16[128,1,128]{2,1,0:T(2,128)(2,1)S(1)} %get-tuple-element.35), channel_id=1, source_target_pairs={{4,0},{8,4},{12,8},{16,12},{20,16},{24,20},{28,24},{5,1},{9,5},{13... | collective-permute-start | bytes 98312 | tf_op jit(solution)/shard_map/ppermute | solution.py:17
  82.6 7.4 %collective-permute-start.2 = (bf16[128,1,128]{2,1,0:T(2,128)(2,1)S(1)}, bf16[128,1,128]{2,1,0:T(2,128)(2,1)S(1)}, u32[]{:S(2)}, u32[]{:S(2)}) collective-permute-start(bf16[128,1,128]{2,1,0:T(2,128)(2,1)S(1)} %get-tuple-element.34), channel_id=1, source_target_pairs={{0,4},{4,8},{8,12},{12,16},{16,20},{20,24},{24,28},{1,5},{5,9},{9,... | collective-permute-start | bytes 98312 | tf_op jit(solution)/shard_map/ppermute | solution.py:15
  99.3 4.3 %copy-start = (bf16[512,6,128]{0,2,1:T(8,128)(2,1)}, bf16[512,6,128]{0,2,1:T(8,128)(2,1)S(1)}, u32[]{:S(2)}) copy-start(bf16[512,6,128]{0,2,1:T(8,128)(2,1)S(1)} %copy.92) | copy-start | bytes 2359300
  103.6 232.9 %all-reduce.49.cloned.1.call-start = ((), (), s32[]{:S(2)}) async-start(), calls=%async_computation.1 | async-start | bytes 4718592 | tf_op jit(solution)/shard_map/psum | solution.py:121
  103.8 6.7 %collective-permute-start.9 = (bf16[128,1,128]{2,1,0:T(2,128)(2,1)S(1)}, bf16[128,1,128]{2,1,0:T(2,128)(2,1)S(1)}, u32[]{:S(2)}, u32[]{:S(2)}) collective-permute-start(bf16[128,1,128]{2,1,0:T(2,128)(2,1)S(1)} %get-tuple-element.32), channel_id=1, source_target_pairs={{0,4},{4,8},{8,12},{12,16},{16,20},{20,24},{24,28},{1,5},{5,9},{9,... | collective-permute-start | bytes 98312 | tf_op jit(solution)/shard_map/ppermute | solution.py:15
  108.6 9.0 %collective-permute-start.8 = (bf16[128,1,128]{2,1,0:T(2,128)(2,1)S(1)}, bf16[128,1,128]{2,1,0:T(2,128)(2,1)S(1)}, u32[]{:S(2)}, u32[]{:S(2)}) collective-permute-start(bf16[128,1,128]{2,1,0:T(2,128)(2,1)S(1)} %get-tuple-element.33), channel_id=1, source_target_pairs={{4,0},{8,4},{12,8},{16,12},{20,16},{24,20},{28,24},{5,1},{9,5},{13... | collective-permute-start | bytes 98312 | tf_op jit(solution)/shard_map/ppermute | solution.py:17
  119.2 96.4 %copy-start.6 = (bf16[128,9,4,128]{3,2,0,1:T(4,128)(2,1)}, bf16[128,9,4,128]{3,2,0,1:T(4,128)(2,1)S(1)}, u32[]{:S(2)}) copy-start(bf16[128,9,4,128]{3,2,0,1:T(4,128)(2,1)S(1)} %bitcast_dynamic-update-slice_fusion.19) | copy-start | bytes 3538948
  228.5 1.3 copy-start.7
  229.9 1.3 copy-start.3
  235.8 11.4 %collective-permute-start.10 = (f32[2,128,4,128]{3,2,1,0:T(4,128)}, f32[2,128,4,128]{3,2,1,0:T(4,128)}, u32[]{:S(2)}, u32[]{:S(2)}) collective-permute-start(f32[2,128,4,128]{3,2,1,0:T(4,128)} %bitcast.46), channel_id=1, source_target_pairs={{0,1},{1,0},{2,3},{3,2},{4,5},{5,4},{6,7},{7,6},{8,9},{9,8},{10,11... | collective-permute-start | bytes 1572872 | tf_op jit(solution)/shard_map/ppermute | solution.py:97
  241.6 4.9 %copy-start.5 = (f32[2,1,128,4,128]{2,1,0,4,3:T(1,128)S(1)}, f32[2,1,128,4,128]{2,1,0,4,3:T(1,128)}, u32[]{:S(2)}) copy-start(f32[2,1,128,4,128]{2,1,0,4,3:T(1,128)} %get-tuple-element.22) | copy-start | bytes 1572868
  248.4 8.8 %collective-permute-start.11 = (f32[1,128,4,128]{3,2,1,0:T(4,128)S(1)}, f32[1,128,4,128]{3,2,1,0:T(4,128)S(1)}, u32[]{:S(2)}, u32[]{:S(2)}) collective-permute-start(f32[1,128,4,128]{3,2,1,0:T(4,128)S(1)} %constant_dynamic-slice_fusion), channel_id=1, source_target_pairs={{0,2},{1,3},{2,0},{3,1},{4,6},{5,7},{6,4},{7,5},{8,10},{9,11},{10,... | collective-permute-start | bytes 786440 | tf_op jit(solution)/shard_map/ppermute | solution.py:97
  252.2 0.9 copy-start.8
  252.7 4.5 %copy-start.9 = (bf16[128,4,128]{2,1,0:T(4,128)(2,1)S(1)}, bf16[128,4,128]{2,1,0:T(4,128)(2,1)}, u32[]{:S(2)}) copy-start(bf16[128,4,128]{2,1,0:T(4,128)(2,1)} %param.7) | copy-start | bytes 393220
  258.0 81.8 %copy-start.4 = (f32[128,3,3,512]{3,0,2,1:T(8,128)S(1)}, f32[128,3,3,512]{3,0,2,1:T(8,128)}, u32[]{:S(2)}) copy-start(f32[128,3,3,512]{3,0,2,1:T(8,128)} %all-reduce.47.cloned.1.call-done) | copy-start | bytes 7077892
Sparse Core Ops, SparseCore 0:
  103.7 111.7 all-reduce.46
  228.7 107.7 all-reduce.48
where the time goes:
time: 349 us; the launch traced here: 348 us
  waiting for transfers between devices  190 us (54%)
  local copies, waits for them, and re-layouts  70.9 us (20%)
  starting transfers between devices  28.7 us (8%)
  blocking collectives  17.7 us (5%)
  matrix products  16.6 us (5%)
  between operations  14.5 us (4%)
  other arithmetic  10 us (3%)
    psum x1, waiting for transfers between devices, body(): second_grad = lax.psum(filter_grad(out_grad, h_all), 'strip')  96.3 us
    psum x1, waiting for transfers between devices, body(): first_grad = lax.psum(filter_grad(late_grad, x_all), 'strip')  78.5 us
    unnamed x52, local copies, waits for them, and re-layouts  26.1 us
    ppermute x4, starting transfers between devices, extended(): lax.ppermute(tail, axis, [(i, (i + 1) % count) for i in range(ends)])  20.3 us
    reshape x2, local copies, waits for them, and re-layouts, conv_fwd(): taps = taps.reshape(outs, 3, 3, rows_pad, cols)  9.65 us
    all_gather x1, blocking collectives, body(): x_all = lax.all_gather(x_pad, 'chan', axis=0, tiled=True)  8.87 us
    all_gather x1, blocking collectives, body(): h_all = lax.all_gather(h_pad, 'chan', axis=0, tiled=True)  8.81 us
    dot_general x2, local copies, waits for them, and re-layouts, conv_fwd(): jnp.dot(flat_w, padded.reshape(chans, rows_pad * cols), preferred_element...  8.26 us
  transfers between devices with their start and end apart: 14, of which 7 were waited for; matrix products, arithmetic and copies ran while one was open for 20% of the time, Pallas kernels for 0%

commit v1 on v0

--- a/solution.py
+++ b/solution.py
@@ -105,7 +105,15 @@
     dy_stack = back_stack(dy_pad)
     hidden_grad = chan_sum_scatter(conv_back_stacked(dy_stack, second_filters, rows, cols), "chan")
     x_pad = extended(features, (("strip", 1),), 1)
-    x_all = lax.all_gather(x_pad, "chan", axis=0, tiled=True)
+    ways, here = (lax.axis_size("chan"), lax.axis_index("chan"))
+    grown, reach = (x_pad, 1)
+    while reach < ways:
+        theirs = lax.ppermute(grown, "chan", [(d, d ^ reach) for d in range(ways)])
+        mine_first = jnp.concatenate([grown, theirs], axis=0)
+        theirs_first = jnp.concatenate([theirs, grown], axis=0)
+        grown = jnp.where(here & reach == 0, mine_first, theirs_first)
+        reach = 2 * reach
+    x_all = grown
     pre_full = conv_fwd(x_all, first_filters)
     pre = pre_full.astype(jnp.bfloat16)
     hidden = jax.nn.silu(pre_full).astype(jnp.bfloat16)

time: 349 us -> 331 us (0.948)
  local copies, waits for them, and re-layouts: 70.9 us -> 59.8 us
  blocking collectives: 17.7 us -> 8.81 us
    all_gather x1 -> x0, blocking collectives: 8.87 us -> none  [body(): x_all = lax.all_gather(x_pad, 'chan', axis=0, tiled=True)]
    ppermute x0 -> x2, waiting for transfers between devices: none -> 8.12 us  [body(): theirs = lax.ppermute(grown, 'chan', [(d, d ^ reach) for d in range(ways)])]
    unnamed x52 -> x68, local copies, waits for them, and re-layouts: 26.1 us -> 20.2 us
    ppermute x4, waiting for transfers between devices: 5.8 us -> 1.5 us  [chan_sum_scatter(): lax.ppermute(send, axis, [(i, i ^ bit) for i in range(count)])]
    psum x1, waiting for transfers between devices: 96.3 us -> 92.6 us  [body(): second_grad = lax.psum(filter_grad(out_grad, h_all), 'strip')]
  transfers between devices with their start and end apart: 14 -> 16, of which waited for: 7 -> 8; matrix products, arithmetic and copies ran while one was open for 20% -> 20% of each run, Pallas kernels for 0% -> 0%
where the time goes in v1:
time: 331 us; the launch traced here: 330 us
  waiting for transfers between devices  189 us (57%)
  local copies, waits for them, and re-layouts  59.8 us (18%)
  starting transfers between devices  29.8 us (9%)
  matrix products  16.2 us (5%)
  between operations  14.7 us (4%)
  other arithmetic  11.9 us (4%)
  blocking collectives  8.81 us (3%)
    psum x1, waiting for transfers between devices, body(): second_grad = lax.psum(filter_grad(out_grad, h_all), 'strip')  92.6 us
    psum x1, waiting for transfers between devices, body(): first_grad = lax.psum(filter_grad(late_grad, x_all), 'strip')  76.9 us
    ppermute x4, starting transfers between devices, extended(): lax.ppermute(tail, axis, [(i, (i + 1) % count) for i in range(ends)])  20.3 us
    unnamed x68, local copies, waits for them, and re-layouts  20.2 us
    all_gather x1, blocking collectives, body(): h_all = lax.all_gather(h_pad, 'chan', axis=0, tiled=True)  8.81 us
    ppermute x2, waiting for transfers between devices, body(): theirs = lax.ppermute(grown, 'chan', [(d, d ^ reach) for d in range(ways)])  8.12 us
    reshape x2, local copies, waits for them, and re-layouts, conv_fwd(): taps = taps.reshape(outs, 3, 3, rows_pad, cols)  7.57 us
    ppermute x4, waiting for transfers between devices, extended(): lax.ppermute(head, axis, [((i + 1) % count, i) for i in range(ends)])  7.4 us
  transfers between devices with their start and end apart: 16, of which 8 were waited for; matrix products, arithmetic and copies ran while one was open for 20% of the time, Pallas kernels for 0%

profile of v1, /device:TPU:0, one launch (start us, length us, event | category | flops | bytes accessed | tf_op | source)
XLA Modules:
  0.0 329.8 jit_solution(7052360698702688692)
XLA Ops:
  8.3 4.8 %collective-permute-start.7 = (bf16[128,1,128]{0,2,1:T(8,128)(2,1)S(1)}, bf16[128,1,128]{0,2,1:T(8,128)(2,1)S(1)}, u32[]{:S(2)}, u32[]{:S(2)}) collective-permute-start(bf16[128,1,128]{0,2,1:T(8,128)(2,1)S(1)} %get-tuple-element.42), channel_id=1, source_target_pairs={{0,4},{4,8},{8,12},{12,16},{16,20},{20,24},{24,28},{1,5},{5,9},{9,... | collective-permute-start | bytes 98312 | tf_op jit(solution)/shard_map/ppermute | solution.py:15
  16.8 5.2 %collective-permute-start = (bf16[128,1,128]{0,2,1:T(8,128)(2,1)S(1)}, bf16[128,1,128]{0,2,1:T(8,128)(2,1)S(1)}, u32[]{:S(2)}, u32[]{:S(2)}) collective-permute-start(bf16[128,1,128]{0,2,1:T(8,128)(2,1)S(1)} %get-tuple-element.36), channel_id=1, source_target_pairs={{0,4},{4,8},{8,12},{12,16},{16,20},{20,24},{24,28},{1,5},{5,9},{9,... | collective-permute-start | bytes 98312 | tf_op jit(solution)/shard_map/ppermute | solution.py:15
  22.0 2.3 copy.93
  25.4 2.7 copy.80
  32.7 3.1 convolution_bitcast_fusion.3
  46.4 8.1 %collective-permute-done.3 = bf16[256,6,128]{0,2,1:T(8,128)(2,1)S(1)} collective-permute-done((bf16[256,6,128]{0,2,1:T(8,128)(2,1)S(1)}, bf16[256,6,128]{0,2,1:T(8,128)(2,1)S(1)}, u32[]{:S(2)}, u32[]{:S(2)}) %collective-permute-start.3) | collective-permute-done | bytes 393248 | tf_op jit(solution)/shard_map/ppermute | solution.py:111
  55.3 3.0 convolution_bitcast_fusion.1
  58.3 3.3 copy.81
  61.6 2.7 reshape.67
  71.4 5.5 %collective-permute-start.4 = (bf16[128,1,128]{2,1,0:T(2,128)(2,1)S(1)}, bf16[128,1,128]{2,1,0:T(2,128)(2,1)S(1)}, u32[]{:S(2)}, u32[]{:S(2)}) collective-permute-start(bf16[128,1,128]{2,1,0:T(2,128)(2,1)S(1)} %get-tuple-element.34), channel_id=1, source_target_pairs={{0,4},{4,8},{8,12},{12,16},{16,20},{20,24},{24,28},{1,5},{5,9},{9,... | collective-permute-start | bytes 98312 | tf_op jit(solution)/shard_map/ppermute | solution.py:15
  79.0 8.8 %all_gather.3 = bf16[512,6,128]{2,0,1:T(8,128)(2,1)S(1)} all-gather(bf16[128,6,128]{2,0,1:T(8,128)(2,1)S(1)} %copy.91), channel_id=1, replica_groups=mesh['strip'=8,'chan'=4] {'chan'}, dimensions={0}, use_global_device_ids=true | all-gather | bytes 983040 | tf_op jit(solution)/shard_map/all_gather | solution.py:121
  88.1 2.5 fusion.76
  90.8 4.8 %collective-permute-start.11 = (bf16[128,1,128]{2,1,0:T(2,128)(2,1)S(1)}, bf16[128,1,128]{2,1,0:T(2,128)(2,1)S(1)}, u32[]{:S(2)}, u32[]{:S(2)}) collective-permute-start(bf16[128,1,128]{2,1,0:T(2,128)(2,1)S(1)} %get-tuple-element.32), channel_id=1, source_target_pairs={{0,4},{4,8},{8,12},{12,16},{16,20},{20,24},{24,28},{1,5},{5,9},{9,... | collective-permute-start | bytes 98312 | tf_op jit(solution)/shard_map/ppermute | solution.py:15
  97.6 7.2 %collective-permute-done.10 = bf16[128,1,128]{2,1,0:T(2,128)(2,1)S(1)} collective-permute-done((bf16[128,1,128]{2,1,0:T(2,128)(2,1)S(1)}, bf16[128,1,128]{2,1,0:T(2,128)(2,1)S(1)}, u32[]{:S(2)}, u32[]{:S(2)}) %collective-permute-start.10) | collective-permute-done | bytes 32800 | tf_op jit(solution)/shard_map/ppermute | solution.py:17
  110.0 92.6 %all-reduce.47.cloned.1.call-done = f32[128,3,3,512]{3,0,2,1:T(8,128)} async-done(((f32[128,3,3,512]{3,0,2,1:T(8,128)}), f32[128,3,3,512]{3,0,2,1:T(8,128)}) %all-reduce.47.cloned.1.call-update) | async-done | bytes 2359312 | tf_op jit(solution)/shard_map/psum | solution.py:122
  203.9 2.4 copy.121
  206.4 4.0 %fusion.4 = f32[128,3,3,512]{3,0,2,1:T(8,128)} fusion(bf16[128,3,3,768]{0,3,2,1:T(8,128)(2,1)} %bitcast.265, bf16[256,768]{0,1:T(8,128)(2,1)S(1)} %bitcast.278, bf16[256,768]{0,1:T(8,128)(2,1)S(1)} %copy-done.15, pred[]{:T(512)S(6)} %eq.11), kind=kOutput, calls=%fused_computation.9 | convolution fusion | flops 909508608 | bytes 4915201 | tf_op jit(solution)/shard_map/dot_general | solution.py:78
  219.2 2.7 convolution_bitcast_fusion
  221.9 3.1 copy.94
  225.0 4.9 %reshape.70 = f32[128,3,3,6,128]{4,3,2,1,0:T(8,128)} reshape(f32[1152,768]{1,0:T(8,128)} %copy.94) | data formatting | bytes 7077888 | tf_op jit(solution)/shard_map/reshape | solution.py:41
  233.4 2.3 slice_bitcast_fusion.8
  236.6 2.6 fusion.23
  241.4 76.9 %all-reduce.49.cloned.1.call-done = f32[128,3,3,512]{3,0,2,1:T(8,128)} async-done(((f32[128,3,3,512]{3,0,2,1:T(8,128)}), f32[128,3,3,512]{3,0,2,1:T(8,128)}) %all-reduce.49.cloned.1.call-update) | async-done | bytes 2359312 | tf_op jit(solution)/shard_map/psum | solution.py:129
  318.3 3.3 copy.190
  (145 shorter events, 56.5 us)
Async XLA Ops:
  7.2 195.4 %all-reduce.47.cloned.1.call-start = ((), (), s32[]{:S(2)}) async-start(), calls=%async_computation | async-start | bytes 4718592 | tf_op jit(solution)/shard_map/psum | solution.py:122
  8.3 22.0 %collective-permute-start.7 = (bf16[128,1,128]{0,2,1:T(8,128)(2,1)S(1)}, bf16[128,1,128]{0,2,1:T(8,128)(2,1)S(1)}, u32[]{:S(2)}, u32[]{:S(2)}) collective-permute-start(bf16[128,1,128]{0,2,1:T(8,128)(2,1)S(1)} %get-tuple-element.42), channel_id=1, source_target_pairs={{0,4},{4,8},{8,12},{12,16},{16,20},{20,24},{24,28},{1,5},{5,9},{9,... | collective-permute-start | bytes 98312 | tf_op jit(solution)/shard_map/ppermute | solution.py:15
  13.1 17.2 %collective-permute-start.6 = (bf16[128,1,128]{0,2,1:T(8,128)(2,1)S(1)}, bf16[128,1,128]{0,2,1:T(8,128)(2,1)S(1)}, u32[]{:S(2)}, u32[]{:S(2)}) collective-permute-start(bf16[128,1,128]{0,2,1:T(8,128)(2,1)S(1)} %get-tuple-element.43), channel_id=1, source_target_pairs={{4,0},{8,4},{12,8},{16,12},{20,16},{24,20},{28,24},{5,1},{9,5},{13... | collective-permute-start | bytes 98312 | tf_op jit(solution)/shard_map/ppermute | solution.py:17
  15.5 24.8 %collective-permute-start.1 = (bf16[128,1,128]{0,2,1:T(8,128)(2,1)S(1)}, bf16[128,1,128]{0,2,1:T(8,128)(2,1)S(1)}, u32[]{:S(2)}, u32[]{:S(2)}) collective-permute-start(bf16[128,1,128]{0,2,1:T(8,128)(2,1)S(1)} %get-tuple-element.37), channel_id=1, source_target_pairs={{4,0},{8,4},{12,8},{16,12},{20,16},{24,20},{28,24},{5,1},{9,5},{13... | collective-permute-start | bytes 98312 | tf_op jit(solution)/shard_map/ppermute | solution.py:17
  16.8 23.5 %collective-permute-start = (bf16[128,1,128]{0,2,1:T(8,128)(2,1)S(1)}, bf16[128,1,128]{0,2,1:T(8,128)(2,1)S(1)}, u32[]{:S(2)}, u32[]{:S(2)}) collective-permute-start(bf16[128,1,128]{0,2,1:T(8,128)(2,1)S(1)} %get-tuple-element.36), channel_id=1, source_target_pairs={{0,4},{4,8},{8,12},{12,16},{16,20},{20,24},{24,28},{1,5},{5,9},{9,... | collective-permute-start | bytes 98312 | tf_op jit(solution)/shard_map/ppermute | solution.py:15
  25.3 7.3 %copy-start.1 = (bf16[1152,512]{1,0:T(8,128)(2,1)}, bf16[1152,512]{1,0:T(8,128)(2,1)S(1)}, u32[]{:S(2)}) copy-start(bf16[1152,512]{1,0:T(8,128)(2,1)S(1)} %reshape.69) | copy-start | bytes 3538948
  39.4 4.8 %collective-permute-start.8 = (f32[2,128,4,128]{3,2,1,0:T(4,128)S(1)}, f32[2,128,4,128]{3,2,1,0:T(4,128)S(1)}, u32[]{:S(2)}, u32[]{:S(2)}) collective-permute-start(f32[2,128,4,128]{3,2,1,0:T(4,128)S(1)} %bitcast.276), channel_id=1, source_target_pairs={{0,1},{1,0},{2,3},{3,2},{4,5},{5,4},{6,7},{7,6},{8,9},{9,8},{10,11... | collective-permute-start | bytes 1572872 | tf_op jit(solution)/shard_map/ppermute | solution.py:97
  40.3 2.1 collective-permute-start.2
  42.5 12.8 %copy-start.10 = (bf16[1152,512]{1,0:T(8,128)(2,1)S(1)}, bf16[1152,512]{1,0:T(8,128)(2,1)}, u32[]{:S(2)}) copy-start(bf16[1152,512]{1,0:T(8,128)(2,1)} %reshape.66) | copy-start | bytes 3538948
  42.5 12.0 %collective-permute-start.3 = (bf16[256,6,128]{0,2,1:T(8,128)(2,1)S(1)}, bf16[256,6,128]{0,2,1:T(8,128)(2,1)S(1)}, u32[]{:S(2)}, u32[]{:S(2)}) collective-permute-start(bf16[256,6,128]{0,2,1:T(8,128)(2,1)S(1)} %maximum_select_fusion.2), channel_id=1, source_target_pairs={{0,2},{1,3},{2,0},{3,1},{4,6},{5,7},{6,4},{7,5},{8,10},{9,11},{10,... | collective-permute-start | bytes 1179656 | tf_op jit(solution)/shard_map/ppermute | solution.py:111
  44.2 10.3 %copy-start.14 = (bf16[256,768]{0,1:T(8,128)(2,1)}, bf16[256,768]{0,1:T(8,128)(2,1)S(1)}, u32[]{:S(2)}) copy-start(bf16[256,768]{0,1:T(8,128)(2,1)S(1)} %maximum_select_fusion.1) | copy-start | bytes 1179652
  45.9 21.3 %collective-permute-start.9 = (f32[1,128,4,128]{3,2,1,0:T(4,128)}, f32[1,128,4,128]{3,2,1,0:T(4,128)}, u32[]{:S(2)}, u32[]{:S(2)}) collective-permute-start(f32[1,128,4,128]{3,2,1,0:T(4,128)} %constant_dynamic-slice_fusion.3), channel_id=1, source_target_pairs={{0,2},{1,3},{2,0},{3,1},{4,6},{5,7},{6,4},{7,5},{8,10},{9,11},{10,... | collective-permute-start | bytes 786440 | tf_op jit(solution)/shard_map/ppermute | solution.py:97
  67.6 9.3 %copy-start.4 = (bf16[128,9,6,128]{0,3,2,1:T(8,128)(2,1)S(1)}, bf16[128,9,6,128]{0,3,2,1:T(8,128)(2,1)}, u32[]{:S(2)}) copy-start(bf16[128,9,6,128]{0,3,2,1:T(8,128)(2,1)} %copy-done.3) | copy-start | bytes 5308420
  67.6 9.3 %copy-start.8 = (bf16[128,4,128]{0,2,1:T(8,128)(2,1)S(1)}, bf16[128,4,128]{0,2,1:T(8,128)(2,1)}, u32[]{:S(2)}) copy-start(bf16[128,4,128]{0,2,1:T(8,128)(2,1)} %copy-done.7) | copy-start | bytes 393220
  70.1 7.1 %collective-permute-start.5 = (bf16[128,1,128]{2,1,0:T(2,128)(2,1)S(1)}, bf16[128,1,128]{2,1,0:T(2,128)(2,1)S(1)}, u32[]{:S(2)}, u32[]{:S(2)}) collective-permute-start(bf16[128,1,128]{2,1,0:T(2,128)(2,1)S(1)} %get-tuple-element.35), channel_id=1, source_target_pairs={{4,0},{8,4},{12,8},{16,12},{20,16},{24,20},{28,24},{5,1},{9,5},{13... | collective-permute-start | bytes 98312 | tf_op jit(solution)/shard_map/ppermute | solution.py:17
  71.4 7.3 %collective-permute-start.4 = (bf16[128,1,128]{2,1,0:T(2,128)(2,1)S(1)}, bf16[128,1,128]{2,1,0:T(2,128)(2,1)S(1)}, u32[]{:S(2)}, u32[]{:S(2)}) collective-permute-start(bf16[128,1,128]{2,1,0:T(2,128)(2,1)S(1)} %get-tuple-element.34), channel_id=1, source_target_pairs={{0,4},{4,8},{8,12},{12,16},{16,20},{20,24},{24,28},{1,5},{5,9},{9,... | collective-permute-start | bytes 98312 | tf_op jit(solution)/shard_map/ppermute | solution.py:15
  90.7 227.6 %all-reduce.49.cloned.1.call-start = ((), (), s32[]{:S(2)}) async-start(), calls=%async_computation.1 | async-start | bytes 4718592 | tf_op jit(solution)/shard_map/psum | solution.py:129
  90.8 6.7 %collective-permute-start.11 = (bf16[128,1,128]{2,1,0:T(2,128)(2,1)S(1)}, bf16[128,1,128]{2,1,0:T(2,128)(2,1)S(1)}, u32[]{:S(2)}, u32[]{:S(2)}) collective-permute-start(bf16[128,1,128]{2,1,0:T(2,128)(2,1)S(1)} %get-tuple-element.32), channel_id=1, source_target_pairs={{0,4},{4,8},{8,12},{12,16},{16,20},{20,24},{24,28},{1,5},{5,9},{9,... | collective-permute-start | bytes 98312 | tf_op jit(solution)/shard_map/ppermute | solution.py:15
  95.7 9.0 %collective-permute-start.10 = (bf16[128,1,128]{2,1,0:T(2,128)(2,1)S(1)}, bf16[128,1,128]{2,1,0:T(2,128)(2,1)S(1)}, u32[]{:S(2)}, u32[]{:S(2)}) collective-permute-start(bf16[128,1,128]{2,1,0:T(2,128)(2,1)S(1)} %get-tuple-element.33), channel_id=1, source_target_pairs={{4,0},{8,4},{12,8},{16,12},{20,16},{24,20},{28,24},{5,1},{9,5},{13... | collective-permute-start | bytes 98312 | tf_op jit(solution)/shard_map/ppermute | solution.py:17
  219.2 11.4 %collective-permute-start.12 = (f32[2,128,4,128]{3,2,1,0:T(4,128)}, f32[2,128,4,128]{3,2,1,0:T(4,128)}, u32[]{:S(2)}, u32[]{:S(2)}) collective-permute-start(f32[2,128,4,128]{3,2,1,0:T(4,128)} %bitcast.48), channel_id=1, source_target_pairs={{0,1},{1,0},{2,3},{3,2},{4,5},{5,4},{6,7},{7,6},{8,9},{9,8},{10,11... | collective-permute-start | bytes 1572872 | tf_op jit(solution)/shard_map/ppermute | solution.py:97
  225.0 4.9 %copy-start.9 = (f32[2,1,128,4,128]{2,1,0,4,3:T(1,128)S(1)}, f32[2,1,128,4,128]{2,1,0,4,3:T(1,128)}, u32[]{:S(2)}) copy-start(f32[2,1,128,4,128]{2,1,0,4,3:T(1,128)} %get-tuple-element.22) | copy-start | bytes 1572868
  231.8 8.8 %collective-permute-start.13 = (f32[1,128,4,128]{3,2,1,0:T(4,128)S(1)}, f32[1,128,4,128]{3,2,1,0:T(4,128)S(1)}, u32[]{:S(2)}, u32[]{:S(2)}) collective-permute-start(f32[1,128,4,128]{3,2,1,0:T(4,128)S(1)} %constant_dynamic-slice_fusion), channel_id=1, source_target_pairs={{0,2},{1,3},{2,0},{3,1},{4,6},{5,7},{6,4},{7,5},{8,10},{9,11},{10,... | collective-permute-start | bytes 786440 | tf_op jit(solution)/shard_map/ppermute | solution.py:97
  236.1 4.5 %copy-start.13 = (bf16[128,4,128]{2,1,0:T(4,128)(2,1)S(1)}, bf16[128,4,128]{2,1,0:T(4,128)(2,1)}, u32[]{:S(2)}) copy-start(bf16[128,4,128]{2,1,0:T(4,128)(2,1)} %param.7) | copy-start | bytes 393220
  241.4 80.2 %copy-start.2 = (f32[128,3,3,512]{3,0,2,1:T(8,128)S(1)}, f32[128,3,3,512]{3,0,2,1:T(8,128)}, u32[]{:S(2)}) copy-start(f32[128,3,3,512]{3,0,2,1:T(8,128)} %all-reduce.47.cloned.1.call-done) | copy-start | bytes 7077892
  (10 other events, 17.9 us)
Sparse Core Ops, SparseCore 0:
  90.8 111.7 all-reduce.46
  210.5 107.7 all-reduce.48
